TPU v7x, 512 devices: a whole 4x4x16 slice. The times are simulated.
512 devices in a mesh: seq: 64 (over z, x_hi, core), section: 8 (over y, x_lo).
Axes of the slice: x: 4 (x_hi: 2, x_lo: 2; x = x_hi * 2 + x_lo), y: 4, z: 16, core: 2. Of those that a mesh axis runs over, the one named last changes fastest.
Arguments:
- fwd_input: bfloat16 [8, 16384, 768], P('section', 'seq'), may hold values from -6 to 6
- bwd_input: bfloat16 [8, 16384, 768], P('section', 'seq'), may hold values from -6 to 6
- bwd_cotangent: bfloat16 [8, 16384, 768], P('section', 'seq'), may hold values from -6 to 6
- conv_weight: bfloat16 [8, 2, 3, 768, 384], P('section', None, None, 'seq'), may hold values from -0.125 to 0.125
- proj_weight: bfloat16 [8, 2, 384, 768], P('section', None, 'seq'), may hold values from -0.3125 to 0.3125
Outputs:
- next_input: bfloat16 [8, 16384, 768], P('section', 'seq')
- prev_cotangent: bfloat16 [8, 16384, 768], P('section', 'seq')
All inputs are finite; a program needn't handle non-finite values.
Results may differ from a plain program's by a relative error of at most 0.012.
Values may be sent and summed in bfloat16 or wider, within the bound.
No kernel may reach another device: no remote copies, remote signals or barrier semaphores. Data moves between devices by JAX's collectives and lax.ppermute only.
A program may use at most 64 MiB of HBM per device.

v0:
```python
import jax
import jax.numpy as jnp
from jax import lax
from jax.sharding import Mesh, PartitionSpec as P

BLOCKS = 2
FIRST_DILATION = 128
SEQ = ("z", "xh", "core")


def seq_size(axis):
    if isinstance(axis, tuple):
        size = 1
        for name in axis:
            size *= lax.axis_size(name)
        return size
    return lax.axis_size(axis)


def padded(x, sides, width):
    for axis, dim in sides:
        size, length = (seq_size(axis), x.shape[dim])
        up = [(i, (i + 1) % size) for i in range(size - 1)]
        down = [(j, i) for i, j in up]
        last = lax.slice_in_dim(x, length - width, length, axis=dim)
        initial = lax.slice_in_dim(x, 0, width, axis=dim)
        before = lax.ppermute(last, axis, up)
        after = lax.ppermute(initial, axis, down)
        x = jnp.concatenate([before, x, after], axis=dim)
    return x


def from_behind(block, axis, distance):
    devices = range(seq_size(axis))
    route = [(i - distance, i) for i in devices if i - distance in devices]
    return lax.ppermute(block, axis, route)


def from_behind_2(block, axis, distance):
    devices = range(seq_size(axis))
    route = [((i - distance) % len(devices), i) for i in devices]
    return lax.ppermute(block, axis, route)


def gelu_back(value, cotangent):
    return jax.vjp(jax.nn.gelu, value)[1](cotangent)[0]


def rounded(product):
    return lax.optimization_barrier(product.astype(jnp.bfloat16)).astype(jnp.float32)


def reach(values, spacing_gap):
    length = values.shape[1]
    if spacing_gap < length:
        padded_input = padded(values, ((SEQ, 1),), spacing_gap)
        return (padded_input[:, :length], padded_input[:, 2 * spacing_gap :])
    shard_hops = spacing_gap // length
    earlier = from_behind(values, SEQ, shard_hops)
    later = from_behind(values, SEQ, -shard_hops)
    return (earlier, later)


def conv_apply(values, weight):
    return jnp.einsum("krc,ch->krh", values, weight, preferred_element_type=jnp.float32)


def conv_transpose(values, weight):
    return jnp.einsum("krh,ch->krc", values, weight, preferred_element_type=jnp.float32)


def run_forward(present_state, pieces):
    stored = []
    for depth_level in range(BLOCKS):
        conv_part, proj_part = pieces[depth_level]
        spacing_gap = FIRST_DILATION * 4**depth_level
        activated = jax.nn.gelu(present_state.astype(jnp.float32)).astype(jnp.bfloat16)
        middle = conv_apply(activated, conv_part[1])
        first_tap = conv_apply(activated, conv_part[0]).astype(jnp.bfloat16)
        last_tap = conv_apply(activated, conv_part[2]).astype(jnp.bfloat16)
        earlier, unused_later = reach(first_tap, spacing_gap)
        unused_earlier, later = reach(last_tap, spacing_gap)
        preact = (
            lax.optimization_barrier(earlier).astype(jnp.float32)
            + middle
            + lax.optimization_barrier(later).astype(jnp.float32)
        )
        hidden = jax.nn.gelu(preact).astype(jnp.bfloat16)
        stored.append((present_state, preact))
        branch = jnp.einsum("krh,hc->krc", hidden, proj_part, preferred_element_type=jnp.float32)
        present_state = (present_state.astype(jnp.float32) + branch).astype(jnp.bfloat16)
    return (present_state, stored)


def place(conv, proj, block, chip, conv_shape, proj_shape):
    rows, split = (block.shape[0], 1)
    for size in conv_shape:
        split *= size
    part = block[:, :split].reshape((rows,) + conv_shape[1:])
    part = jnp.moveaxis(part, 0, 2).reshape(conv_shape[:3] + (rows * conv_shape[3], conv_shape[4]))
    conv = lax.dynamic_update_slice(conv, part, (0, 0, 0, chip * rows * conv_shape[3], 0))
    part = block[:, split:].reshape((rows,) + proj_shape[1:])
    part = jnp.moveaxis(part, 0, 1).reshape(proj_shape[:2] + (rows * proj_shape[2], proj_shape[3]))
    proj = lax.dynamic_update_slice(proj, part, (0, 0, chip * rows * proj_shape[2], 0))
    return (conv, proj)


def gather_weights(conv_weight, proj_weight):
    conv_shape, proj_shape = (conv_weight.shape, proj_weight.shape)
    block = jnp.concatenate([conv_weight.reshape(1, -1), proj_weight.reshape(1, -1)], axis=1)
    block = lax.all_gather(block, "core", axis=0, tiled=True)
    block = lax.all_gather(block, "xh", axis=0, tiled=True)
    span, lanes, cores = (lax.axis_size("z"), lax.axis_size("xh"), lax.axis_size("core"))
    here, core = (lax.axis_index("z"), lax.axis_index("core"))
    sign = 2 * core - 1
    route = []
    for z in range(span):
        for x in range(lanes):
            route.append(((z * lanes + x) * cores, ((z + 1) % span * lanes + x) * cores))
            route.append(((z * lanes + x) * cores + 1, ((z - 1) % span * lanes + x) * cores + 1))
    shards = span * lanes * cores
    conv = jnp.zeros(conv_shape[:3] + (shards * conv_shape[3], conv_shape[4]), conv_weight.dtype)
    proj = jnp.zeros(proj_shape[:2] + (shards * proj_shape[2], proj_shape[3]), proj_weight.dtype)
    conv, proj = place(conv, proj, block, here, conv_shape, proj_shape)
    half = span // 2
    current = block
    for step in range(1, half + 1):
        current = lax.ppermute(current, SEQ, route)
        conv, proj = place(conv, proj, current, (here + sign * step) % span, conv_shape, proj_shape)
        if step < span - half:
            peer = lax.ppermute(current, "core", [(0, 1), (1, 0)])
            conv, proj = place(
                conv, proj, peer, (here - sign * step) % span, conv_shape, proj_shape
            )
    return (conv, proj)


def local(fwd_input, bwd_input, bwd_cotangent, conv_weight, proj_weight):
    convolution_complete, proj_full = gather_weights(conv_weight, proj_weight)
    pieces = [
        (convolution_complete[0, depth_level], proj_full[0, depth_level])
        for depth_level in range(BLOCKS)
    ]
    both_out, both_stored = run_forward(jnp.concatenate([fwd_input, bwd_input], axis=0), pieces)
    forward_out = both_out[:1]
    stored = [(block_in[1:], preact[1:]) for block_in, preact in both_stored]
    cotangent = bwd_cotangent
    for depth_level in reversed(range(BLOCKS)):
        conv_part, proj_part = pieces[depth_level]
        spacing_gap = FIRST_DILATION * 4**depth_level
        block_in, preact = stored[depth_level]
        d_hidden = jnp.einsum(
            "krc,hc->krh", cotangent, proj_part, preferred_element_type=jnp.float32
        )
        d_preact = gelu_back(preact, d_hidden).astype(jnp.bfloat16)
        earlier, later = reach(d_preact, spacing_gap)
        d_act = (
            conv_transpose(later, conv_part[0])
            + conv_transpose(d_preact, conv_part[1])
            + conv_transpose(earlier, conv_part[2])
        )
        total = cotangent.astype(jnp.float32) + gelu_back(block_in.astype(jnp.float32), d_act)
        cotangent = total.astype(jnp.bfloat16)
    next_input = from_behind_2(forward_out, "section", 1)
    prev_cotangent = from_behind_2(cotangent, "section", -1)
    return (next_input, prev_cotangent)


def solution(mesh):
    seq, section = (mesh.shape["seq"], mesh.shape["section"])
    split = Mesh(mesh.devices.reshape(seq // 4, 2, 2, section), SEQ + ("section",))
    in_specs = (
        P("section", SEQ, None),
        P("section", SEQ, None),
        P("section", SEQ, None),
        P("section", None, None, SEQ, None),
        P("section", None, SEQ, None),
    )
    out_specs = (P("section", SEQ, None), P("section", SEQ, None))
    return jax.shard_map(local, mesh=split, in_specs=in_specs, out_specs=out_specs, check_vma=False)
```

profile of v0, /device:TPU:127, one launch (start us, length us, event | category | flops | bytes accessed | tf_op | source)
XLA Modules:
  0.0 322.7 jit_solution(8147360253637598649)
XLA Ops:
  2.4 2.3 all-gather
  5.0 7.2 %all-gather.1 = bf16[2,2,36864]{2,1,0:T(2,128)(2,1)S(1)} all-gather(bf16[1,2,36864]{2,1,0:T(2,128)(2,1)S(1)} %bitcast.209), channel_id=1, replica_groups=mesh['z'=16,'xh'=2,'core'=2,'section'=8] {'xh'}, dimensions={0}, use_global_device_ids=true | all-gather | bytes 442368 | tf_op jit(solution)/shard_map/all_gather | solution.py:112
  13.0 1.9 collective-permute-start
  26.2 1.9 collective-permute-start.2
  28.2 7.2 %collective-permute-start.1 = (bf16[4,36864]{1,0:T(4,128)(2,1)}, bf16[4,36864]{1,0:T(4,128)(2,1)}, u32[]{:S(2)}, u32[]{:S(2)}) collective-permute-start(bf16[4,36864]{1,0:T(4,128)(2,1)} %collective-permute-done), channel_id=1, source_target_pairs={{0,8},{8,0},{1,9},{9,1},{2,10},{10,2},{3,11},{11,3},{4,12},{12,4},... | collective-permute-start | bytes 884744 | tf_op jit(solution)/shard_map/ppermute | solution.py:131
  36.0 1.7 slice.233
  37.7 1.8 reshape.254
  50.1 1.7 slice.234
  51.8 1.8 reshape.256
  56.4 1.9 collective-permute-start.4
  58.3 3.3 %collective-permute-start.3 = (bf16[4,36864]{1,0:T(4,128)(2,1)}, bf16[4,36864]{1,0:T(4,128)(2,1)}, u32[]{:S(2)}, u32[]{:S(2)}) collective-permute-start(bf16[4,36864]{1,0:T(4,128)(2,1)} %collective-permute-done.2), channel_id=1, source_target_pairs={{0,8},{8,0},{1,9},{9,1},{2,10},{10,2},{3,11},{11,3},{4,12},{12,4},... | collective-permute-start | bytes 884744 | tf_op jit(solution)/shard_map/ppermute | solution.py:131
  63.2 1.7 slice.235
  64.9 1.8 reshape.258
  77.3 1.7 slice.236
  79.0 1.8 reshape.260
  83.5 2.4 collective-permute-start.6
  85.9 3.4 %collective-permute-start.5 = (bf16[4,36864]{1,0:T(4,128)(2,1)}, bf16[4,36864]{1,0:T(4,128)(2,1)}, u32[]{:S(2)}, u32[]{:S(2)}) collective-permute-start(bf16[4,36864]{1,0:T(4,128)(2,1)} %collective-permute-done.4), channel_id=1, source_target_pairs={{0,8},{8,0},{1,9},{9,1},{2,10},{10,2},{3,11},{11,3},{4,12},{12,4},... | collective-permute-start | bytes 884744 | tf_op jit(solution)/shard_map/ppermute | solution.py:131
  90.9 1.7 slice.237
  92.6 1.8 reshape.262
  105.0 1.7 slice.238
  106.7 1.8 reshape.264
  111.2 1.9 collective-permute-start.8
  113.1 4.9 %collective-permute-start.7 = (bf16[4,36864]{1,0:T(4,128)(2,1)}, bf16[4,36864]{1,0:T(4,128)(2,1)}, u32[]{:S(2)}, u32[]{:S(2)}) collective-permute-start(bf16[4,36864]{1,0:T(4,128)(2,1)} %collective-permute-done.6), channel_id=1, source_target_pairs={{0,8},{8,0},{1,9},{9,1},{2,10},{10,2},{3,11},{11,3},{4,12},{12,4},... | collective-permute-start | bytes 884744 | tf_op jit(solution)/shard_map/ppermute | solution.py:131
  119.6 1.7 slice.239
  121.3 1.8 reshape.266
  133.7 1.7 slice.240
  135.4 1.8 reshape.268
  139.9 1.9 collective-permute-start.10
  141.8 4.3 %collective-permute-start.9 = (bf16[4,36864]{1,0:T(4,128)(2,1)}, bf16[4,36864]{1,0:T(4,128)(2,1)}, u32[]{:S(2)}, u32[]{:S(2)}) collective-permute-start(bf16[4,36864]{1,0:T(4,128)(2,1)} %collective-permute-done.8), channel_id=1, source_target_pairs={{0,8},{8,0},{1,9},{9,1},{2,10},{10,2},{3,11},{11,3},{4,12},{12,4},... | collective-permute-start | bytes 884744 | tf_op jit(solution)/shard_map/ppermute | solution.py:131
  147.7 1.7 slice.241
  149.4 1.8 reshape.270
  161.8 1.7 slice.242
  163.5 1.8 reshape.272
  168.0 1.9 collective-permute-start.12
  169.9 3.1 collective-permute-start.11
  176.3 1.8 reshape.274
  190.3 1.8 reshape.276
  194.9 2.6 collective-permute-start.14
  197.5 3.7 %collective-permute-start.13 = (bf16[4,36864]{1,0:T(4,128)(2,1)}, bf16[4,36864]{1,0:T(4,128)(2,1)}, u32[]{:S(2)}, u32[]{:S(2)}) collective-permute-start(bf16[4,36864]{1,0:T(4,128)(2,1)} %collective-permute-done.12), channel_id=1, source_target_pairs={{0,8},{8,0},{1,9},{9,1},{2,10},{10,2},{3,11},{11,3},{4,12},{12,4},... | collective-permute-start | bytes 884744 | tf_op jit(solution)/shard_map/ppermute | solution.py:131
  202.7 1.7 slice.245
  204.4 1.8 reshape.278
  207.4 1.7 slice.247
  209.1 1.8 reshape.282
  210.9 1.8 copy.107
  212.7 1.7 slice.246
  214.4 1.8 reshape.280
  218.4 2.6 convolution_convert_fusion.3
  233.9 3.4 %collective-permute-start.15 = (bf16[2,128,384]{2,1,0:T(8,128)(2,1)S(1)}, bf16[2,128,384]{2,1,0:T(8,128)(2,1)S(1)}, u32[]{:S(2)}, u32[]{:S(2)}) collective-permute-start(bf16[2,128,384]{2,1,0:T(8,128)(2,1)S(1)} %slice.249), channel_id=1, source_target_pairs={{0,8},{8,16},{16,24},{24,32},{32,40},{40,48},{48,56},{56,64},{64,7... | collective-permute-start | bytes 589832 | tf_op jit(solution)/shard_map/ppermute | solution.py:27
  238.3 1.9 collective-permute-start.16
  243.4 5.5 %collective-permute-done.16 = bf16[2,128,384]{2,1,0:T(8,128)(2,1)S(1)} collective-permute-done((bf16[2,128,384]{2,1,0:T(8,128)(2,1)S(1)}, bf16[2,128,384]{2,1,0:T(8,128)(2,1)S(1)}, u32[]{:S(2)}, u32[]{:S(2)}) %collective-permute-start.16) | collective-permute-done | bytes 196640 | tf_op jit(solution)/shard_map/ppermute | solution.py:28
  249.1 1.7 fusion.156
  251.5 1.9 collective-permute-start.17
  254.2 4.9 %collective-permute-start.18 = (bf16[2,256,384]{2,1,0:T(8,128)(2,1)S(1)}, bf16[2,256,384]{2,1,0:T(8,128)(2,1)S(1)}, u32[]{:S(2)}, u32[]{:S(2)}) collective-permute-start(bf16[2,256,384]{2,1,0:T(8,128)(2,1)S(1)} %convolution_convert_fusion), channel_id=1, source_target_pairs={{16,0},{24,8},{32,16},{40,24},{48,32},{56,40},{64,48},{72,56},{80,... | collective-permute-start | bytes 1179656 | tf_op jit(solution)/shard_map/ppermute | solution.py:36
  259.8 12.1 %collective-permute-done.17 = bf16[2,256,384]{2,1,0:T(8,128)(2,1)S(1)} collective-permute-done((bf16[2,256,384]{2,1,0:T(8,128)(2,1)S(1)}, bf16[2,256,384]{2,1,0:T(8,128)(2,1)S(1)}, u32[]{:S(2)}, u32[]{:S(2)}) %collective-permute-start.17) | collective-permute-done | bytes 393248 | tf_op jit(solution)/shard_map/ppermute | solution.py:36
  273.6 6.5 %collective-permute-start.21 = (bf16[1,256,384]{2,1,0:T(8,128)(2,1)S(1)}, bf16[1,256,384]{2,1,0:T(8,128)(2,1)S(1)}, u32[]{:S(2)}, u32[]{:S(2)}) collective-permute-start(bf16[1,256,384]{2,1,0:T(8,128)(2,1)S(1)} %fusion.101), channel_id=1, source_target_pairs={{0,16},{8,24},{16,32},{24,40},{32,48},{40,56},{48,64},{56,72},{64,... | collective-permute-start | bytes 589832 | tf_op jit(solution)/shard_map/ppermute | solution.py:36
  280.1 1.9 collective-permute-start.20
  282.0 1.7 fusion.56
  283.9 2.1 collective-permute-start.19
  286.8 4.6 %collective-permute-done.20 = bf16[1,256,384]{2,1,0:T(8,128)(2,1)S(1)} collective-permute-done((bf16[1,256,384]{2,1,0:T(8,128)(2,1)S(1)}, bf16[1,256,384]{2,1,0:T(8,128)(2,1)S(1)}, u32[]{:S(2)}, u32[]{:S(2)}) %collective-permute-start.20) | collective-permute-done | bytes 196640 | tf_op jit(solution)/shard_map/ppermute | solution.py:36
  293.8 5.7 %collective-permute-start.23 = (bf16[1,128,384]{2,1,0:T(8,128)(2,1)S(1)}, bf16[1,128,384]{2,1,0:T(8,128)(2,1)S(1)}, u32[]{:S(2)}, u32[]{:S(2)}) collective-permute-start(bf16[1,128,384]{2,1,0:T(8,128)(2,1)S(1)} %get-tuple-element.3), channel_id=1, source_target_pairs={{0,8},{8,16},{16,24},{24,32},{32,40},{40,48},{48,56},{56,64},{64,7... | collective-permute-start | bytes 294920 | tf_op jit(solution)/shard_map/ppermute | solution.py:27
  299.9 1.9 collective-permute-start.22
  302.2 7.2 %collective-permute-done.22 = bf16[1,128,384]{2,1,0:T(8,128)(2,1)S(1)} collective-permute-done((bf16[1,128,384]{2,1,0:T(8,128)(2,1)S(1)}, bf16[1,128,384]{2,1,0:T(8,128)(2,1)S(1)}, u32[]{:S(2)}, u32[]{:S(2)}) %collective-permute-start.22) | collective-permute-done | bytes 98336 | tf_op jit(solution)/shard_map/ppermute | solution.py:28
  310.2 2.2 collective-permute-start.24
  312.4 8.7 %collective-permute-done.24 = bf16[1,256,768]{2,1,0:T(8,128)(2,1)S(1)} collective-permute-done((bf16[1,256,768]{2,1,0:T(8,128)(2,1)S(1)}, bf16[1,256,768]{2,1,0:T(8,128)(2,1)S(1)}, u32[]{:S(2)}, u32[]{:S(2)}) %collective-permute-start.24) | collective-permute-done | bytes 393248 | tf_op jit(solution)/shard_map/ppermute | solution.py:42
  (167 shorter events, 137.7 us)
Async XLA Ops:
  13.0 9.2 %collective-permute-start = (bf16[4,36864]{1,0:T(4,128)(2,1)}, bf16[4,36864]{1,0:T(4,128)(2,1)}, u32[]{:S(2)}, u32[]{:S(2)}) collective-permute-start(bf16[4,36864]{1,0:T(4,128)(2,1)} %reshape.327), channel_id=1, source_target_pairs={{0,32},{8,488},{16,48},{24,504},{32,64},{40,8},{48,80},{56,24},{64... | collective-permute-start | bytes 884744 | tf_op jit(solution)/shard_map/ppermute | solution.py:128
  19.8 0.9 copy-start.1
  26.2 14.5 %collective-permute-start.2 = (bf16[4,36864]{1,0:T(4,128)(2,1)}, bf16[4,36864]{1,0:T(4,128)(2,1)}, u32[]{:S(2)}, u32[]{:S(2)}) collective-permute-start(bf16[4,36864]{1,0:T(4,128)(2,1)} %collective-permute-done), channel_id=1, source_target_pairs={{0,32},{8,488},{16,48},{24,504},{32,64},{40,8},{48,80},{56,24},{64... | collective-permute-start | bytes 884744 | tf_op jit(solution)/shard_map/ppermute | solution.py:128
  28.2 17.3 %collective-permute-start.1 = (bf16[4,36864]{1,0:T(4,128)(2,1)}, bf16[4,36864]{1,0:T(4,128)(2,1)}, u32[]{:S(2)}, u32[]{:S(2)}) collective-permute-start(bf16[4,36864]{1,0:T(4,128)(2,1)} %collective-permute-done), channel_id=1, source_target_pairs={{0,8},{8,0},{1,9},{9,1},{2,10},{10,2},{3,11},{11,3},{4,12},{12,4},... | collective-permute-start | bytes 884744 | tf_op jit(solution)/shard_map/ppermute | solution.py:131
  56.4 11.5 %collective-permute-start.4 = (bf16[4,36864]{1,0:T(4,128)(2,1)}, bf16[4,36864]{1,0:T(4,128)(2,1)}, u32[]{:S(2)}, u32[]{:S(2)}) collective-permute-start(bf16[4,36864]{1,0:T(4,128)(2,1)} %collective-permute-done.2), channel_id=1, source_target_pairs={{0,32},{8,488},{16,48},{24,504},{32,64},{40,8},{48,80},{56,24},{64... | collective-permute-start | bytes 884744 | tf_op jit(solution)/shard_map/ppermute | solution.py:128
  58.3 14.3 %collective-permute-start.3 = (bf16[4,36864]{1,0:T(4,128)(2,1)}, bf16[4,36864]{1,0:T(4,128)(2,1)}, u32[]{:S(2)}, u32[]{:S(2)}) collective-permute-start(bf16[4,36864]{1,0:T(4,128)(2,1)} %collective-permute-done.2), channel_id=1, source_target_pairs={{0,8},{8,0},{1,9},{9,1},{2,10},{10,2},{3,11},{11,3},{4,12},{12,4},... | collective-permute-start | bytes 884744 | tf_op jit(solution)/shard_map/ppermute | solution.py:131
  83.5 12.1 %collective-permute-start.6 = (bf16[4,36864]{1,0:T(4,128)(2,1)}, bf16[4,36864]{1,0:T(4,128)(2,1)}, u32[]{:S(2)}, u32[]{:S(2)}) collective-permute-start(bf16[4,36864]{1,0:T(4,128)(2,1)} %collective-permute-done.4), channel_id=1, source_target_pairs={{0,32},{8,488},{16,48},{24,504},{32,64},{40,8},{48,80},{56,24},{64... | collective-permute-start | bytes 884744 | tf_op jit(solution)/shard_map/ppermute | solution.py:128
  85.9 14.4 %collective-permute-start.5 = (bf16[4,36864]{1,0:T(4,128)(2,1)}, bf16[4,36864]{1,0:T(4,128)(2,1)}, u32[]{:S(2)}, u32[]{:S(2)}) collective-permute-start(bf16[4,36864]{1,0:T(4,128)(2,1)} %collective-permute-done.4), channel_id=1, source_target_pairs={{0,8},{8,0},{1,9},{9,1},{2,10},{10,2},{3,11},{11,3},{4,12},{12,4},... | collective-permute-start | bytes 884744 | tf_op jit(solution)/shard_map/ppermute | solution.py:131
  111.2 13.1 %collective-permute-start.8 = (bf16[4,36864]{1,0:T(4,128)(2,1)}, bf16[4,36864]{1,0:T(4,128)(2,1)}, u32[]{:S(2)}, u32[]{:S(2)}) collective-permute-start(bf16[4,36864]{1,0:T(4,128)(2,1)} %collective-permute-done.6), channel_id=1, source_target_pairs={{0,32},{8,488},{16,48},{24,504},{32,64},{40,8},{48,80},{56,24},{64... | collective-permute-start | bytes 884744 | tf_op jit(solution)/shard_map/ppermute | solution.py:128
  113.1 15.8 %collective-permute-start.7 = (bf16[4,36864]{1,0:T(4,128)(2,1)}, bf16[4,36864]{1,0:T(4,128)(2,1)}, u32[]{:S(2)}, u32[]{:S(2)}) collective-permute-start(bf16[4,36864]{1,0:T(4,128)(2,1)} %collective-permute-done.6), channel_id=1, source_target_pairs={{0,8},{8,0},{1,9},{9,1},{2,10},{10,2},{3,11},{11,3},{4,12},{12,4},... | collective-permute-start | bytes 884744 | tf_op jit(solution)/shard_map/ppermute | solution.py:131
  139.9 12.5 %collective-permute-start.10 = (bf16[4,36864]{1,0:T(4,128)(2,1)}, bf16[4,36864]{1,0:T(4,128)(2,1)}, u32[]{:S(2)}, u32[]{:S(2)}) collective-permute-start(bf16[4,36864]{1,0:T(4,128)(2,1)} %collective-permute-done.8), channel_id=1, source_target_pairs={{0,32},{8,488},{16,48},{24,504},{32,64},{40,8},{48,80},{56,24},{64... | collective-permute-start | bytes 884744 | tf_op jit(solution)/shard_map/ppermute | solution.py:128
  141.8 15.3 %collective-permute-start.9 = (bf16[4,36864]{1,0:T(4,128)(2,1)}, bf16[4,36864]{1,0:T(4,128)(2,1)}, u32[]{:S(2)}, u32[]{:S(2)}) collective-permute-start(bf16[4,36864]{1,0:T(4,128)(2,1)} %collective-permute-done.8), channel_id=1, source_target_pairs={{0,8},{8,0},{1,9},{9,1},{2,10},{10,2},{3,11},{11,3},{4,12},{12,4},... | collective-permute-start | bytes 884744 | tf_op jit(solution)/shard_map/ppermute | solution.py:131
  168.0 11.3 %collective-permute-start.12 = (bf16[4,36864]{1,0:T(4,128)(2,1)}, bf16[4,36864]{1,0:T(4,128)(2,1)}, u32[]{:S(2)}, u32[]{:S(2)}) collective-permute-start(bf16[4,36864]{1,0:T(4,128)(2,1)} %collective-permute-done.10), channel_id=1, source_target_pairs={{0,32},{8,488},{16,48},{24,504},{32,64},{40,8},{48,80},{56,24},{64... | collective-permute-start | bytes 884744 | tf_op jit(solution)/shard_map/ppermute | solution.py:128
  169.9 14.0 %collective-permute-start.11 = (bf16[4,36864]{1,0:T(4,128)(2,1)}, bf16[4,36864]{1,0:T(4,128)(2,1)}, u32[]{:S(2)}, u32[]{:S(2)}) collective-permute-start(bf16[4,36864]{1,0:T(4,128)(2,1)} %collective-permute-done.10), channel_id=1, source_target_pairs={{0,8},{8,0},{1,9},{9,1},{2,10},{10,2},{3,11},{11,3},{4,12},{12,4},... | collective-permute-start | bytes 884744 | tf_op jit(solution)/shard_map/ppermute | solution.py:131
  194.9 12.5 %collective-permute-start.14 = (bf16[4,36864]{1,0:T(4,128)(2,1)}, bf16[4,36864]{1,0:T(4,128)(2,1)}, u32[]{:S(2)}, u32[]{:S(2)}) collective-permute-start(bf16[4,36864]{1,0:T(4,128)(2,1)} %collective-permute-done.12), channel_id=1, source_target_pairs={{0,32},{8,488},{16,48},{24,504},{32,64},{40,8},{48,80},{56,24},{64... | collective-permute-start | bytes 884744 | tf_op jit(solution)/shard_map/ppermute | solution.py:128
  197.5 15.2 %collective-permute-start.13 = (bf16[4,36864]{1,0:T(4,128)(2,1)}, bf16[4,36864]{1,0:T(4,128)(2,1)}, u32[]{:S(2)}, u32[]{:S(2)}) collective-permute-start(bf16[4,36864]{1,0:T(4,128)(2,1)} %collective-permute-done.12), channel_id=1, source_target_pairs={{0,8},{8,0},{1,9},{9,1},{2,10},{10,2},{3,11},{11,3},{4,12},{12,4},... | collective-permute-start | bytes 884744 | tf_op jit(solution)/shard_map/ppermute | solution.py:131
  218.4 2.7 copy-start.3
  218.4 2.7 copy-start.6
  231.9 16.9 %copy-start = (bf16[2,256,384]{2,1,0:T(8,128)(2,1)S(1)}, bf16[2,256,384]{2,1,0:T(8,128)(2,1)}, u32[]{:S(2)}) copy-start(bf16[2,256,384]{2,1,0:T(8,128)(2,1)} %convolution_convert_fusion.2) | copy-start | bytes 1179652
  231.9 17.0 %copy-start.2 = (f32[2,256,384]{2,1,0:T(8,128)S(1)}, f32[2,256,384]{2,1,0:T(8,128)}, u32[]{:S(2)}) copy-start(f32[2,256,384]{2,1,0:T(8,128)} %fusion.64) | copy-start | bytes 2359300
  233.9 8.4 %collective-permute-start.15 = (bf16[2,128,384]{2,1,0:T(8,128)(2,1)S(1)}, bf16[2,128,384]{2,1,0:T(8,128)(2,1)S(1)}, u32[]{:S(2)}, u32[]{:S(2)}) collective-permute-start(bf16[2,128,384]{2,1,0:T(8,128)(2,1)S(1)} %slice.249), channel_id=1, source_target_pairs={{0,8},{8,16},{16,24},{24,32},{32,40},{40,48},{48,56},{56,64},{64,7... | collective-permute-start | bytes 589832 | tf_op jit(solution)/shard_map/ppermute | solution.py:27
  238.3 10.6 %collective-permute-start.16 = (bf16[2,128,384]{2,1,0:T(8,128)(2,1)S(1)}, bf16[2,128,384]{2,1,0:T(8,128)(2,1)S(1)}, u32[]{:S(2)}, u32[]{:S(2)}) collective-permute-start(bf16[2,128,384]{2,1,0:T(8,128)(2,1)S(1)} %slice.252), channel_id=1, source_target_pairs={{8,0},{16,8},{24,16},{32,24},{40,32},{48,40},{56,48},{64,56},{72,6... | collective-permute-start | bytes 589832 | tf_op jit(solution)/shard_map/ppermute | solution.py:28
  243.3 5.7 %copy-start.4 = (bf16[1,256,768]{2,1,0:T(8,128)(2,1)S(1)}, bf16[1,256,768]{2,1,0:T(8,128)(2,1)}, u32[]{:S(2)}) copy-start(bf16[1,256,768]{2,1,0:T(8,128)(2,1)} %param.5) | copy-start | bytes 1179652
  243.4 5.7 %copy-start.7 = (bf16[1,256,768]{2,1,0:T(8,128)(2,1)S(1)}, bf16[1,256,768]{2,1,0:T(8,128)(2,1)}, u32[]{:S(2)}) copy-start(bf16[1,256,768]{2,1,0:T(8,128)(2,1)} %param.6) | copy-start | bytes 1179652
  251.5 20.3 %collective-permute-start.17 = (bf16[2,256,384]{2,1,0:T(8,128)(2,1)S(1)}, bf16[2,256,384]{2,1,0:T(8,128)(2,1)S(1)}, u32[]{:S(2)}, u32[]{:S(2)}) collective-permute-start(bf16[2,256,384]{2,1,0:T(8,128)(2,1)S(1)} %convolution_convert_fusion.1), channel_id=1, source_target_pairs={{0,16},{8,24},{16,32},{24,40},{32,48},{40,56},{48,64},{56,72},{64,... | collective-permute-start | bytes 1179656 | tf_op jit(solution)/shard_map/ppermute | solution.py:36
  254.2 17.7 %collective-permute-start.18 = (bf16[2,256,384]{2,1,0:T(8,128)(2,1)S(1)}, bf16[2,256,384]{2,1,0:T(8,128)(2,1)S(1)}, u32[]{:S(2)}, u32[]{:S(2)}) collective-permute-start(bf16[2,256,384]{2,1,0:T(8,128)(2,1)S(1)} %convolution_convert_fusion), channel_id=1, source_target_pairs={{16,0},{24,8},{32,16},{40,24},{48,32},{56,40},{64,48},{72,56},{80,... | collective-permute-start | bytes 1179656 | tf_op jit(solution)/shard_map/ppermute | solution.py:36
  259.8 12.2 %copy-start.5 = (bf16[1,256,768]{2,1,0:T(8,128)(2,1)S(1)}, bf16[1,256,768]{2,1,0:T(8,128)(2,1)}, u32[]{:S(2)}) copy-start(bf16[1,256,768]{2,1,0:T(8,128)(2,1)} %param.7) | copy-start | bytes 1179652
  273.6 12.8 %collective-permute-start.21 = (bf16[1,256,384]{2,1,0:T(8,128)(2,1)S(1)}, bf16[1,256,384]{2,1,0:T(8,128)(2,1)S(1)}, u32[]{:S(2)}, u32[]{:S(2)}) collective-permute-start(bf16[1,256,384]{2,1,0:T(8,128)(2,1)S(1)} %fusion.101), channel_id=1, source_target_pairs={{0,16},{8,24},{16,32},{24,40},{32,48},{40,56},{48,64},{56,72},{64,... | collective-permute-start | bytes 589832 | tf_op jit(solution)/shard_map/ppermute | solution.py:36
  280.1 11.3 %collective-permute-start.20 = (bf16[1,256,384]{2,1,0:T(8,128)(2,1)S(1)}, bf16[1,256,384]{2,1,0:T(8,128)(2,1)S(1)}, u32[]{:S(2)}, u32[]{:S(2)}) collective-permute-start(bf16[1,256,384]{2,1,0:T(8,128)(2,1)S(1)} %fusion.101), channel_id=1, source_target_pairs={{16,0},{24,8},{32,16},{40,24},{48,32},{56,40},{64,48},{72,56},{80,... | collective-permute-start | bytes 589832 | tf_op jit(solution)/shard_map/ppermute | solution.py:36
  283.9 28.6 %collective-permute-start.19 = (bf16[1,256,768]{2,1,0:T(8,128)(2,1)S(1)}, bf16[1,256,768]{2,1,0:T(8,128)(2,1)S(1)}, u32[]{:S(2)}, u32[]{:S(2)}) collective-permute-start(bf16[1,256,768]{2,1,0:T(8,128)(2,1)S(1)} %fusion.55), channel_id=1, source_target_pairs={{7,0},{0,1},{1,2},{2,3},{3,4},{4,5},{5,6},{6,7},{15,8},{8,9},{9,10... | collective-permute-start | bytes 1179656 | tf_op jit(solution)/shard_map/ppermute | solution.py:42
  293.8 8.0 %collective-permute-start.23 = (bf16[1,128,384]{2,1,0:T(8,128)(2,1)S(1)}, bf16[1,128,384]{2,1,0:T(8,128)(2,1)S(1)}, u32[]{:S(2)}, u32[]{:S(2)}) collective-permute-start(bf16[1,128,384]{2,1,0:T(8,128)(2,1)S(1)} %get-tuple-element.3), channel_id=1, source_target_pairs={{0,8},{8,16},{16,24},{24,32},{32,40},{40,48},{48,56},{56,64},{64,7... | collective-permute-start | bytes 294920 | tf_op jit(solution)/shard_map/ppermute | solution.py:27
  299.9 9.5 %collective-permute-start.22 = (bf16[1,128,384]{2,1,0:T(8,128)(2,1)S(1)}, bf16[1,128,384]{2,1,0:T(8,128)(2,1)S(1)}, u32[]{:S(2)}, u32[]{:S(2)}) collective-permute-start(bf16[1,128,384]{2,1,0:T(8,128)(2,1)S(1)} %get-tuple-element.2), channel_id=1, source_target_pairs={{8,0},{16,8},{24,16},{32,24},{40,32},{48,40},{56,48},{64,56},{72,6... | collective-permute-start | bytes 294920 | tf_op jit(solution)/shard_map/ppermute | solution.py:28
  310.2 10.9 %collective-permute-start.24 = (bf16[1,256,768]{2,1,0:T(8,128)(2,1)S(1)}, bf16[1,256,768]{2,1,0:T(8,128)(2,1)S(1)}, u32[]{:S(2)}, u32[]{:S(2)}) collective-permute-start(bf16[1,256,768]{2,1,0:T(8,128)(2,1)S(1)} %fusion.24), channel_id=1, source_target_pairs={{1,0},{2,1},{3,2},{4,3},{5,4},{6,5},{7,6},{0,7},{9,8},{10,9},{11,1... | collective-permute-start | bytes 1179656 | tf_op jit(solution)/shard_map/ppermute | solution.py:42
where the time goes:
time: 328 us; the launch traced here: 323 us
  local copies, waits for them, and re-layouts  174 us (53%)
  starting transfers between devices  79 us (24%)
  waiting for transfers between devices  39.6 us (12%)
  matrix products  17.6 us (5%)
  blocking collectives  9.53 us (3%)
    ppermute x7, starting transfers between devices, gather_weights(): peer = lax.ppermute(current, 'core', [(0, 1), (1, 0)])  30 us
    reshape x16, local copies, waits for them, and re-layouts, place(): part = block[:, :split].reshape((rows,) + conv_shape[1:])  27.1 us
    slice x16, local copies, waits for them, and re-layouts, place(): part = block[:, :split].reshape((rows,) + conv_shape[1:])  26.5 us
    slice x16, local copies, waits for them, and re-layouts, place(): part = block[:, split:].reshape((rows,) + proj_shape[1:])  24.1 us
    reshape x16, local copies, waits for them, and re-layouts, place(): part = block[:, split:].reshape((rows,) + proj_shape[1:])  23.7 us
    transpose x16, local copies, waits for them, and re-layouts, place(): jnp.moveaxis(part, 0, 1)  22.5 us
    dynamic_update_slice x16, local copies, waits for them, and re-layouts, place(): lax.dynamic_update_slice(proj, part, (0, 0, chip * rows * proj_shape[2], 0))  21.8 us
    transpose x16, local copies, waits for them, and re-layouts, place(): jnp.moveaxis(part, 0, 2)  18.5 us
  transfers between devices with their start and end apart: 25, of which 6 were waited for; matrix products, arithmetic and copies ran while one was open for 29% of the time, Pallas kernels for 0%

commit v1 on v0

--- a/solution.py
+++ b/solution.py
@@ -109,7 +109,9 @@
     conv_shape, proj_shape = (conv_weight.shape, proj_weight.shape)
     block = jnp.concatenate([conv_weight.reshape(1, -1), proj_weight.reshape(1, -1)], axis=1)
     block = lax.all_gather(block, "core", axis=0, tiled=True)
-    block = lax.all_gather(block, "xh", axis=0, tiled=True)
+    block = jnp.concatenate(
+        lax.all_to_all(jnp.stack([block] * lax.axis_size("xh")), "xh", 0, 0), axis=0
+    )
     span, lanes, cores = (lax.axis_size("z"), lax.axis_size("xh"), lax.axis_size("core"))
     here, core = (lax.axis_index("z"), lax.axis_index("core"))
     sign = 2 * core - 1

time: 328 us -> 333 us (1.015)
  starting transfers between devices: 79 us -> 86.9 us
  blocking collectives: 9.53 us -> 2.33 us
  waiting for transfers between devices: 39.6 us -> 44.2 us
    all_gather x1 -> x0, blocking collectives: 7.2 us -> none  [gather_weights(): block = lax.all_gather(block, 'xh', axis=0, tiled=True)]
    all_to_all x0 -> x1, starting transfers between devices: none -> 4.56 us  [gather_weights(): lax.all_to_all(jnp.stack([block] * lax.axis_size('xh')), 'xh', 0, 0)]
    all_to_all x0 -> x1, waiting for transfers between devices: none -> 4.08 us  [gather_weights(): lax.all_to_all(jnp.stack([block] * lax.axis_size('xh')), 'xh', 0, 0)]
  transfers between devices with their start and end apart: 25 -> 26, of which waited for: 6 -> 8; matrix products, arithmetic and copies ran while one was open for 29% -> 28% of each run, Pallas kernels for 0% -> 0%
where the time goes in v1:
time: 333 us; the launch traced here: 328 us
  local copies, waits for them, and re-layouts  173 us (52%)
  starting transfers between devices  86.9 us (26%)
  waiting for transfers between devices  44.2 us (13%)
  matrix products  17.6 us (5%)
    ppermute x7, starting transfers between devices, gather_weights(): peer = lax.ppermute(current, 'core', [(0, 1), (1, 0)])  29 us
    reshape x16, local copies, waits for them, and re-layouts, place(): part = block[:, :split].reshape((rows,) + conv_shape[1:])  27.1 us
    slice x16, local copies, waits for them, and re-layouts, place(): part = block[:, :split].reshape((rows,) + conv_shape[1:])  26.5 us
    slice x16, local copies, waits for them, and re-layouts, place(): part = block[:, split:].reshape((rows,) + proj_shape[1:])  24 us
    reshape x16, local copies, waits for them, and re-layouts, place(): part = block[:, split:].reshape((rows,) + proj_shape[1:])  23.7 us
    transpose x16, local copies, waits for them, and re-layouts, place(): jnp.moveaxis(part, 0, 1)  22.6 us
    dynamic_update_slice x16, local copies, waits for them, and re-layouts, place(): lax.dynamic_update_slice(proj, part, (0, 0, chip * rows * proj_shape[2], 0))  21.8 us
    transpose x16, local copies, waits for them, and re-layouts, place(): jnp.moveaxis(part, 0, 2)  17.9 us
  transfers between devices with their start and end apart: 26, of which 8 were waited for; matrix products, arithmetic and copies ran while one was open for 28% of the time, Pallas kernels for 0%

profile of v1, /device:TPU:127, one launch (start us, length us, event | category | flops | bytes accessed | tf_op | source)
XLA Modules:
  0.0 327.6 jit_solution(8818311237300937818)
XLA Ops:
  2.4 2.3 all-gather
  6.0 4.6 %all-to-all-start = ((bf16[2,2,36864]{2,1,0:T(2,128)(2,1)}), bf16[2,2,36864]{2,1,0:T(2,128)(2,1)S(1)}, u32[]{:S(2)}, u32[]{:S(2)}) async-start(bf16[2,2,36864]{2,1,0:T(2,128)(2,1)} %pad_maximum_fusion.3), calls=%async_computation | async-start | bytes 589824 | tf_op jit(solution)/shard_map/all_to_all | solution.py:113
  10.5 4.1 %all-to-all-done = bf16[2,2,36864]{2,1,0:T(2,128)(2,1)S(1)} async-done(((bf16[2,2,36864]{2,1,0:T(2,128)(2,1)}), bf16[2,2,36864]{2,1,0:T(2,128)(2,1)S(1)}, u32[]{:S(2)}, u32[]{:S(2)}) %all-to-all-start) | async-done | bytes 294944 | tf_op jit(solution)/shard_map/all_to_all | solution.py:113
  16.3 1.9 collective-permute-start
  21.9 3.6 %collective-permute-done = bf16[4,36864]{1,0:T(4,128)(2,1)} collective-permute-done((bf16[4,36864]{1,0:T(4,128)(2,1)}, bf16[4,36864]{1,0:T(4,128)(2,1)}, u32[]{:S(2)}, u32[]{:S(2)}) %collective-permute-start) | collective-permute-done | bytes 294944 | tf_op jit(solution)/shard_map/ppermute | solution.py:130
  29.6 1.9 collective-permute-start.2
  31.5 6.9 %collective-permute-start.1 = (bf16[4,36864]{1,0:T(4,128)(2,1)}, bf16[4,36864]{1,0:T(4,128)(2,1)}, u32[]{:S(2)}, u32[]{:S(2)}) collective-permute-start(bf16[4,36864]{1,0:T(4,128)(2,1)} %collective-permute-done), channel_id=1, source_target_pairs={{0,8},{8,0},{1,9},{9,1},{2,10},{10,2},{3,11},{11,3},{4,12},{12,4},... | collective-permute-start | bytes 884744 | tf_op jit(solution)/shard_map/ppermute | solution.py:133
  39.1 1.7 slice.233
  40.8 1.8 reshape.258
  53.2 1.7 slice.234
  54.9 1.8 reshape.260
  59.4 1.9 collective-permute-start.4
  61.3 2.9 collective-permute-start.3
  65.8 1.7 slice.235
  67.5 1.8 reshape.262
  79.9 1.7 slice.236
  81.5 1.8 reshape.264
  86.1 2.7 collective-permute-start.6
  88.7 3.6 %collective-permute-start.5 = (bf16[4,36864]{1,0:T(4,128)(2,1)}, bf16[4,36864]{1,0:T(4,128)(2,1)}, u32[]{:S(2)}, u32[]{:S(2)}) collective-permute-start(bf16[4,36864]{1,0:T(4,128)(2,1)} %collective-permute-done.4), channel_id=1, source_target_pairs={{0,8},{8,0},{1,9},{9,1},{2,10},{10,2},{3,11},{11,3},{4,12},{12,4},... | collective-permute-start | bytes 884744 | tf_op jit(solution)/shard_map/ppermute | solution.py:133
  93.9 1.7 slice.237
  95.6 1.8 reshape.266
  108.0 1.7 slice.238
  109.7 1.8 reshape.268
  114.2 2.0 collective-permute-start.8
  116.2 3.6 %collective-permute-start.7 = (bf16[4,36864]{1,0:T(4,128)(2,1)}, bf16[4,36864]{1,0:T(4,128)(2,1)}, u32[]{:S(2)}, u32[]{:S(2)}) collective-permute-start(bf16[4,36864]{1,0:T(4,128)(2,1)} %collective-permute-done.6), channel_id=1, source_target_pairs={{0,8},{8,0},{1,9},{9,1},{2,10},{10,2},{3,11},{11,3},{4,12},{12,4},... | collective-permute-start | bytes 884744 | tf_op jit(solution)/shard_map/ppermute | solution.py:133
  121.3 1.7 slice.239
  123.0 1.8 reshape.270
  135.4 1.7 slice.240
  137.1 1.8 reshape.272
  141.6 2.3 collective-permute-start.10
  144.0 5.2 %collective-permute-start.9 = (bf16[4,36864]{1,0:T(4,128)(2,1)}, bf16[4,36864]{1,0:T(4,128)(2,1)}, u32[]{:S(2)}, u32[]{:S(2)}) collective-permute-start(bf16[4,36864]{1,0:T(4,128)(2,1)} %collective-permute-done.8), channel_id=1, source_target_pairs={{0,8},{8,0},{1,9},{9,1},{2,10},{10,2},{3,11},{11,3},{4,12},{12,4},... | collective-permute-start | bytes 884744 | tf_op jit(solution)/shard_map/ppermute | solution.py:133
  152.4 1.8 reshape.274
  166.5 1.8 reshape.276
  171.0 1.9 collective-permute-start.12
  172.9 3.1 collective-permute-start.11
  179.3 1.8 reshape.278
  193.4 1.8 reshape.280
  197.9 2.6 collective-permute-start.14
  200.5 3.6 %collective-permute-start.13 = (bf16[4,36864]{1,0:T(4,128)(2,1)}, bf16[4,36864]{1,0:T(4,128)(2,1)}, u32[]{:S(2)}, u32[]{:S(2)}) collective-permute-start(bf16[4,36864]{1,0:T(4,128)(2,1)} %collective-permute-done.12), channel_id=1, source_target_pairs={{0,8},{8,0},{1,9},{9,1},{2,10},{10,2},{3,11},{11,3},{4,12},{12,4},... | collective-permute-start | bytes 884744 | tf_op jit(solution)/shard_map/ppermute | solution.py:133
  207.4 1.8 reshape.282
  210.4 1.7 slice.247
  212.1 1.8 reshape.286
  213.9 1.8 copy.107
  215.7 1.7 slice.246
  217.4 1.8 reshape.284
  221.4 2.6 convolution_convert_fusion.3
  236.9 5.3 %collective-permute-start.15 = (bf16[2,128,384]{2,1,0:T(8,128)(2,1)S(1)}, bf16[2,128,384]{2,1,0:T(8,128)(2,1)S(1)}, u32[]{:S(2)}, u32[]{:S(2)}) collective-permute-start(bf16[2,128,384]{2,1,0:T(8,128)(2,1)S(1)} %slice.249), channel_id=1, source_target_pairs={{0,8},{8,16},{16,24},{24,32},{32,40},{40,48},{48,56},{56,64},{64,7... | collective-permute-start | bytes 589832 | tf_op jit(solution)/shard_map/ppermute | solution.py:27
  243.1 1.9 collective-permute-start.16
  248.2 5.5 %collective-permute-done.16 = bf16[2,128,384]{2,1,0:T(8,128)(2,1)S(1)} collective-permute-done((bf16[2,128,384]{2,1,0:T(8,128)(2,1)S(1)}, bf16[2,128,384]{2,1,0:T(8,128)(2,1)S(1)}, u32[]{:S(2)}, u32[]{:S(2)}) %collective-permute-start.16) | collective-permute-done | bytes 196640 | tf_op jit(solution)/shard_map/ppermute | solution.py:28
  253.9 1.7 fusion.156
  256.4 1.9 collective-permute-start.17
  259.0 4.9 %collective-permute-start.18 = (bf16[2,256,384]{2,1,0:T(8,128)(2,1)S(1)}, bf16[2,256,384]{2,1,0:T(8,128)(2,1)S(1)}, u32[]{:S(2)}, u32[]{:S(2)}) collective-permute-start(bf16[2,256,384]{2,1,0:T(8,128)(2,1)S(1)} %convolution_convert_fusion), channel_id=1, source_target_pairs={{16,0},{24,8},{32,16},{40,24},{48,32},{56,40},{64,48},{72,56},{80,... | collective-permute-start | bytes 1179656 | tf_op jit(solution)/shard_map/ppermute | solution.py:36
  264.6 2.4 collective-permute-done.17
  267.0 7.9 %collective-permute-done.18 = bf16[2,256,384]{2,1,0:T(8,128)(2,1)S(1)} collective-permute-done((bf16[2,256,384]{2,1,0:T(8,128)(2,1)S(1)}, bf16[2,256,384]{2,1,0:T(8,128)(2,1)S(1)}, u32[]{:S(2)}, u32[]{:S(2)}) %collective-permute-start.18) | collective-permute-done | bytes 393248 | tf_op jit(solution)/shard_map/ppermute | solution.py:36
  276.6 8.3 %collective-permute-start.21 = (bf16[1,256,384]{2,1,0:T(8,128)(2,1)S(1)}, bf16[1,256,384]{2,1,0:T(8,128)(2,1)S(1)}, u32[]{:S(2)}, u32[]{:S(2)}) collective-permute-start(bf16[1,256,384]{2,1,0:T(8,128)(2,1)S(1)} %fusion.101), channel_id=1, source_target_pairs={{0,16},{8,24},{16,32},{24,40},{32,48},{40,56},{48,64},{56,72},{64,... | collective-permute-start | bytes 589832 | tf_op jit(solution)/shard_map/ppermute | solution.py:36
  285.0 1.9 collective-permute-start.20
  286.9 1.7 fusion.56
  288.7 2.1 collective-permute-start.19
  291.7 4.6 %collective-permute-done.20 = bf16[1,256,384]{2,1,0:T(8,128)(2,1)S(1)} collective-permute-done((bf16[1,256,384]{2,1,0:T(8,128)(2,1)S(1)}, bf16[1,256,384]{2,1,0:T(8,128)(2,1)S(1)}, u32[]{:S(2)}, u32[]{:S(2)}) %collective-permute-start.20) | collective-permute-done | bytes 196640 | tf_op jit(solution)/shard_map/ppermute | solution.py:36
  298.7 5.7 %collective-permute-start.23 = (bf16[1,128,384]{2,1,0:T(8,128)(2,1)S(1)}, bf16[1,128,384]{2,1,0:T(8,128)(2,1)S(1)}, u32[]{:S(2)}, u32[]{:S(2)}) collective-permute-start(bf16[1,128,384]{2,1,0:T(8,128)(2,1)S(1)} %get-tuple-element.3), channel_id=1, source_target_pairs={{0,8},{8,16},{16,24},{24,32},{32,40},{40,48},{48,56},{56,64},{64,7... | collective-permute-start | bytes 294920 | tf_op jit(solution)/shard_map/ppermute | solution.py:27
  304.8 1.9 collective-permute-start.22
  307.1 7.3 %collective-permute-done.22 = bf16[1,128,384]{2,1,0:T(8,128)(2,1)S(1)} collective-permute-done((bf16[1,128,384]{2,1,0:T(8,128)(2,1)S(1)}, bf16[1,128,384]{2,1,0:T(8,128)(2,1)S(1)}, u32[]{:S(2)}, u32[]{:S(2)}) %collective-permute-start.22) | collective-permute-done | bytes 98336 | tf_op jit(solution)/shard_map/ppermute | solution.py:28
  315.2 2.1 collective-permute-start.24
  317.3 8.7 %collective-permute-done.24 = bf16[1,256,768]{2,1,0:T(8,128)(2,1)S(1)} collective-permute-done((bf16[1,256,768]{2,1,0:T(8,128)(2,1)S(1)}, bf16[1,256,768]{2,1,0:T(8,128)(2,1)S(1)}, u32[]{:S(2)}, u32[]{:S(2)}) %collective-permute-start.24) | collective-permute-done | bytes 393248 | tf_op jit(solution)/shard_map/ppermute | solution.py:42
  (167 shorter events, 140.9 us)
Async XLA Ops:
  6.0 8.6 %all-to-all-start = ((bf16[2,2,36864]{2,1,0:T(2,128)(2,1)}), bf16[2,2,36864]{2,1,0:T(2,128)(2,1)S(1)}, u32[]{:S(2)}, u32[]{:S(2)}) async-start(bf16[2,2,36864]{2,1,0:T(2,128)(2,1)} %pad_maximum_fusion.3), calls=%async_computation | async-start | bytes 589824 | tf_op jit(solution)/shard_map/all_to_all | solution.py:113
  16.3 9.2 %collective-permute-start = (bf16[4,36864]{1,0:T(4,128)(2,1)}, bf16[4,36864]{1,0:T(4,128)(2,1)}, u32[]{:S(2)}, u32[]{:S(2)}) collective-permute-start(bf16[4,36864]{1,0:T(4,128)(2,1)} %reshape.255), channel_id=1, source_target_pairs={{0,32},{8,488},{16,48},{24,504},{32,64},{40,8},{48,80},{56,24},{64... | collective-permute-start | bytes 884744 | tf_op jit(solution)/shard_map/ppermute | solution.py:130
  29.6 14.2 %collective-permute-start.2 = (bf16[4,36864]{1,0:T(4,128)(2,1)}, bf16[4,36864]{1,0:T(4,128)(2,1)}, u32[]{:S(2)}, u32[]{:S(2)}) collective-permute-start(bf16[4,36864]{1,0:T(4,128)(2,1)} %collective-permute-done), channel_id=1, source_target_pairs={{0,32},{8,488},{16,48},{24,504},{32,64},{40,8},{48,80},{56,24},{64... | collective-permute-start | bytes 884744 | tf_op jit(solution)/shard_map/ppermute | solution.py:130
  31.5 17.0 %collective-permute-start.1 = (bf16[4,36864]{1,0:T(4,128)(2,1)}, bf16[4,36864]{1,0:T(4,128)(2,1)}, u32[]{:S(2)}, u32[]{:S(2)}) collective-permute-start(bf16[4,36864]{1,0:T(4,128)(2,1)} %collective-permute-done), channel_id=1, source_target_pairs={{0,8},{8,0},{1,9},{9,1},{2,10},{10,2},{3,11},{11,3},{4,12},{12,4},... | collective-permute-start | bytes 884744 | tf_op jit(solution)/shard_map/ppermute | solution.py:133
  59.4 11.0 %collective-permute-start.4 = (bf16[4,36864]{1,0:T(4,128)(2,1)}, bf16[4,36864]{1,0:T(4,128)(2,1)}, u32[]{:S(2)}, u32[]{:S(2)}) collective-permute-start(bf16[4,36864]{1,0:T(4,128)(2,1)} %collective-permute-done.2), channel_id=1, source_target_pairs={{0,32},{8,488},{16,48},{24,504},{32,64},{40,8},{48,80},{56,24},{64... | collective-permute-start | bytes 884744 | tf_op jit(solution)/shard_map/ppermute | solution.py:130
  61.3 13.8 %collective-permute-start.3 = (bf16[4,36864]{1,0:T(4,128)(2,1)}, bf16[4,36864]{1,0:T(4,128)(2,1)}, u32[]{:S(2)}, u32[]{:S(2)}) collective-permute-start(bf16[4,36864]{1,0:T(4,128)(2,1)} %collective-permute-done.2), channel_id=1, source_target_pairs={{0,8},{8,0},{1,9},{9,1},{2,10},{10,2},{3,11},{11,3},{4,12},{12,4},... | collective-permute-start | bytes 884744 | tf_op jit(solution)/shard_map/ppermute | solution.py:133
  86.1 12.5 %collective-permute-start.6 = (bf16[4,36864]{1,0:T(4,128)(2,1)}, bf16[4,36864]{1,0:T(4,128)(2,1)}, u32[]{:S(2)}, u32[]{:S(2)}) collective-permute-start(bf16[4,36864]{1,0:T(4,128)(2,1)} %collective-permute-done.4), channel_id=1, source_target_pairs={{0,32},{8,488},{16,48},{24,504},{32,64},{40,8},{48,80},{56,24},{64... | collective-permute-start | bytes 884744 | tf_op jit(solution)/shard_map/ppermute | solution.py:130
  88.7 14.6 %collective-permute-start.5 = (bf16[4,36864]{1,0:T(4,128)(2,1)}, bf16[4,36864]{1,0:T(4,128)(2,1)}, u32[]{:S(2)}, u32[]{:S(2)}) collective-permute-start(bf16[4,36864]{1,0:T(4,128)(2,1)} %collective-permute-done.4), channel_id=1, source_target_pairs={{0,8},{8,0},{1,9},{9,1},{2,10},{10,2},{3,11},{11,3},{4,12},{12,4},... | collective-permute-start | bytes 884744 | tf_op jit(solution)/shard_map/ppermute | solution.py:133
  114.2 11.8 %collective-permute-start.8 = (bf16[4,36864]{1,0:T(4,128)(2,1)}, bf16[4,36864]{1,0:T(4,128)(2,1)}, u32[]{:S(2)}, u32[]{:S(2)}) collective-permute-start(bf16[4,36864]{1,0:T(4,128)(2,1)} %collective-permute-done.6), channel_id=1, source_target_pairs={{0,32},{8,488},{16,48},{24,504},{32,64},{40,8},{48,80},{56,24},{64... | collective-permute-start | bytes 884744 | tf_op jit(solution)/shard_map/ppermute | solution.py:130
  116.2 14.5 %collective-permute-start.7 = (bf16[4,36864]{1,0:T(4,128)(2,1)}, bf16[4,36864]{1,0:T(4,128)(2,1)}, u32[]{:S(2)}, u32[]{:S(2)}) collective-permute-start(bf16[4,36864]{1,0:T(4,128)(2,1)} %collective-permute-done.6), channel_id=1, source_target_pairs={{0,8},{8,0},{1,9},{9,1},{2,10},{10,2},{3,11},{11,3},{4,12},{12,4},... | collective-permute-start | bytes 884744 | tf_op jit(solution)/shard_map/ppermute | solution.py:133
  141.6 13.7 %collective-permute-start.10 = (bf16[4,36864]{1,0:T(4,128)(2,1)}, bf16[4,36864]{1,0:T(4,128)(2,1)}, u32[]{:S(2)}, u32[]{:S(2)}) collective-permute-start(bf16[4,36864]{1,0:T(4,128)(2,1)} %collective-permute-done.8), channel_id=1, source_target_pairs={{0,32},{8,488},{16,48},{24,504},{32,64},{40,8},{48,80},{56,24},{64... | collective-permute-start | bytes 884744 | tf_op jit(solution)/shard_map/ppermute | solution.py:130
  144.0 16.1 %collective-permute-start.9 = (bf16[4,36864]{1,0:T(4,128)(2,1)}, bf16[4,36864]{1,0:T(4,128)(2,1)}, u32[]{:S(2)}, u32[]{:S(2)}) collective-permute-start(bf16[4,36864]{1,0:T(4,128)(2,1)} %collective-permute-done.8), channel_id=1, source_target_pairs={{0,8},{8,0},{1,9},{9,1},{2,10},{10,2},{3,11},{11,3},{4,12},{12,4},... | collective-permute-start | bytes 884744 | tf_op jit(solution)/shard_map/ppermute | solution.py:133
  171.0 11.3 %collective-permute-start.12 = (bf16[4,36864]{1,0:T(4,128)(2,1)}, bf16[4,36864]{1,0:T(4,128)(2,1)}, u32[]{:S(2)}, u32[]{:S(2)}) collective-permute-start(bf16[4,36864]{1,0:T(4,128)(2,1)} %collective-permute-done.10), channel_id=1, source_target_pairs={{0,32},{8,488},{16,48},{24,504},{32,64},{40,8},{48,80},{56,24},{64... | collective-permute-start | bytes 884744 | tf_op jit(solution)/shard_map/ppermute | solution.py:130
  172.9 14.0 %collective-permute-start.11 = (bf16[4,36864]{1,0:T(4,128)(2,1)}, bf16[4,36864]{1,0:T(4,128)(2,1)}, u32[]{:S(2)}, u32[]{:S(2)}) collective-permute-start(bf16[4,36864]{1,0:T(4,128)(2,1)} %collective-permute-done.10), channel_id=1, source_target_pairs={{0,8},{8,0},{1,9},{9,1},{2,10},{10,2},{3,11},{11,3},{4,12},{12,4},... | collective-permute-start | bytes 884744 | tf_op jit(solution)/shard_map/ppermute | solution.py:133
  197.9 12.5 %collective-permute-start.14 = (bf16[4,36864]{1,0:T(4,128)(2,1)}, bf16[4,36864]{1,0:T(4,128)(2,1)}, u32[]{:S(2)}, u32[]{:S(2)}) collective-permute-start(bf16[4,36864]{1,0:T(4,128)(2,1)} %collective-permute-done.12), channel_id=1, source_target_pairs={{0,32},{8,488},{16,48},{24,504},{32,64},{40,8},{48,80},{56,24},{64... | collective-permute-start | bytes 884744 | tf_op jit(solution)/shard_map/ppermute | solution.py:130
  200.5 15.2 %collective-permute-start.13 = (bf16[4,36864]{1,0:T(4,128)(2,1)}, bf16[4,36864]{1,0:T(4,128)(2,1)}, u32[]{:S(2)}, u32[]{:S(2)}) collective-permute-start(bf16[4,36864]{1,0:T(4,128)(2,1)} %collective-permute-done.12), channel_id=1, source_target_pairs={{0,8},{8,0},{1,9},{9,1},{2,10},{10,2},{3,11},{11,3},{4,12},{12,4},... | collective-permute-start | bytes 884744 | tf_op jit(solution)/shard_map/ppermute | solution.py:133
  221.4 2.7 copy-start.2
  221.4 2.7 copy-start.5
  234.9 18.8 %copy-start = (bf16[2,256,384]{2,1,0:T(8,128)(2,1)S(1)}, bf16[2,256,384]{2,1,0:T(8,128)(2,1)}, u32[]{:S(2)}) copy-start(bf16[2,256,384]{2,1,0:T(8,128)(2,1)} %convolution_convert_fusion.2) | copy-start | bytes 1179652
  234.9 18.9 %copy-start.1 = (f32[2,256,384]{2,1,0:T(8,128)S(1)}, f32[2,256,384]{2,1,0:T(8,128)}, u32[]{:S(2)}) copy-start(f32[2,256,384]{2,1,0:T(8,128)} %fusion.64) | copy-start | bytes 2359300
  236.9 10.3 %collective-permute-start.15 = (bf16[2,128,384]{2,1,0:T(8,128)(2,1)S(1)}, bf16[2,128,384]{2,1,0:T(8,128)(2,1)S(1)}, u32[]{:S(2)}, u32[]{:S(2)}) collective-permute-start(bf16[2,128,384]{2,1,0:T(8,128)(2,1)S(1)} %slice.249), channel_id=1, source_target_pairs={{0,8},{8,16},{16,24},{24,32},{32,40},{40,48},{48,56},{56,64},{64,7... | collective-permute-start | bytes 589832 | tf_op jit(solution)/shard_map/ppermute | solution.py:27
  243.1 10.6 %collective-permute-start.16 = (bf16[2,128,384]{2,1,0:T(8,128)(2,1)S(1)}, bf16[2,128,384]{2,1,0:T(8,128)(2,1)S(1)}, u32[]{:S(2)}, u32[]{:S(2)}) collective-permute-start(bf16[2,128,384]{2,1,0:T(8,128)(2,1)S(1)} %slice.252), channel_id=1, source_target_pairs={{8,0},{16,8},{24,16},{32,24},{40,32},{48,40},{56,48},{64,56},{72,6... | collective-permute-start | bytes 589832 | tf_op jit(solution)/shard_map/ppermute | solution.py:28
  248.2 5.7 %copy-start.3 = (bf16[1,256,768]{2,1,0:T(8,128)(2,1)S(1)}, bf16[1,256,768]{2,1,0:T(8,128)(2,1)}, u32[]{:S(2)}) copy-start(bf16[1,256,768]{2,1,0:T(8,128)(2,1)} %param.5) | copy-start | bytes 1179652
  248.2 5.7 %copy-start.6 = (bf16[1,256,768]{2,1,0:T(8,128)(2,1)S(1)}, bf16[1,256,768]{2,1,0:T(8,128)(2,1)}, u32[]{:S(2)}) copy-start(bf16[1,256,768]{2,1,0:T(8,128)(2,1)} %param.6) | copy-start | bytes 1179652
  256.4 10.6 %collective-permute-start.17 = (bf16[2,256,384]{2,1,0:T(8,128)(2,1)S(1)}, bf16[2,256,384]{2,1,0:T(8,128)(2,1)S(1)}, u32[]{:S(2)}, u32[]{:S(2)}) collective-permute-start(bf16[2,256,384]{2,1,0:T(8,128)(2,1)S(1)} %convolution_convert_fusion.1), channel_id=1, source_target_pairs={{0,16},{8,24},{16,32},{24,40},{32,48},{40,56},{48,64},{56,72},{64,... | collective-permute-start | bytes 1179656 | tf_op jit(solution)/shard_map/ppermute | solution.py:36
  259.0 15.9 %collective-permute-start.18 = (bf16[2,256,384]{2,1,0:T(8,128)(2,1)S(1)}, bf16[2,256,384]{2,1,0:T(8,128)(2,1)S(1)}, u32[]{:S(2)}, u32[]{:S(2)}) collective-permute-start(bf16[2,256,384]{2,1,0:T(8,128)(2,1)S(1)} %convolution_convert_fusion), channel_id=1, source_target_pairs={{16,0},{24,8},{32,16},{40,24},{48,32},{56,40},{64,48},{72,56},{80,... | collective-permute-start | bytes 1179656 | tf_op jit(solution)/shard_map/ppermute | solution.py:36
  264.6 10.4 %copy-start.4 = (bf16[1,256,768]{2,1,0:T(8,128)(2,1)S(1)}, bf16[1,256,768]{2,1,0:T(8,128)(2,1)}, u32[]{:S(2)}) copy-start(bf16[1,256,768]{2,1,0:T(8,128)(2,1)} %param.7) | copy-start | bytes 1179652
  276.6 14.6 %collective-permute-start.21 = (bf16[1,256,384]{2,1,0:T(8,128)(2,1)S(1)}, bf16[1,256,384]{2,1,0:T(8,128)(2,1)S(1)}, u32[]{:S(2)}, u32[]{:S(2)}) collective-permute-start(bf16[1,256,384]{2,1,0:T(8,128)(2,1)S(1)} %fusion.101), channel_id=1, source_target_pairs={{0,16},{8,24},{16,32},{24,40},{32,48},{40,56},{48,64},{56,72},{64,... | collective-permute-start | bytes 589832 | tf_op jit(solution)/shard_map/ppermute | solution.py:36
  285.0 11.3 %collective-permute-start.20 = (bf16[1,256,384]{2,1,0:T(8,128)(2,1)S(1)}, bf16[1,256,384]{2,1,0:T(8,128)(2,1)S(1)}, u32[]{:S(2)}, u32[]{:S(2)}) collective-permute-start(bf16[1,256,384]{2,1,0:T(8,128)(2,1)S(1)} %fusion.101), channel_id=1, source_target_pairs={{16,0},{24,8},{32,16},{40,24},{48,32},{56,40},{64,48},{72,56},{80,... | collective-permute-start | bytes 589832 | tf_op jit(solution)/shard_map/ppermute | solution.py:36
  288.7 28.6 %collective-permute-start.19 = (bf16[1,256,768]{2,1,0:T(8,128)(2,1)S(1)}, bf16[1,256,768]{2,1,0:T(8,128)(2,1)S(1)}, u32[]{:S(2)}, u32[]{:S(2)}) collective-permute-start(bf16[1,256,768]{2,1,0:T(8,128)(2,1)S(1)} %fusion.55), channel_id=1, source_target_pairs={{7,0},{0,1},{1,2},{2,3},{3,4},{4,5},{5,6},{6,7},{15,8},{8,9},{9,10... | collective-permute-start | bytes 1179656 | tf_op jit(solution)/shard_map/ppermute | solution.py:42
  298.7 8.0 %collective-permute-start.23 = (bf16[1,128,384]{2,1,0:T(8,128)(2,1)S(1)}, bf16[1,128,384]{2,1,0:T(8,128)(2,1)S(1)}, u32[]{:S(2)}, u32[]{:S(2)}) collective-permute-start(bf16[1,128,384]{2,1,0:T(8,128)(2,1)S(1)} %get-tuple-element.3), channel_id=1, source_target_pairs={{0,8},{8,16},{16,24},{24,32},{32,40},{40,48},{48,56},{56,64},{64,7... | collective-permute-start | bytes 294920 | tf_op jit(solution)/shard_map/ppermute | solution.py:27
  304.8 9.6 %collective-permute-start.22 = (bf16[1,128,384]{2,1,0:T(8,128)(2,1)S(1)}, bf16[1,128,384]{2,1,0:T(8,128)(2,1)S(1)}, u32[]{:S(2)}, u32[]{:S(2)}) collective-permute-start(bf16[1,128,384]{2,1,0:T(8,128)(2,1)S(1)} %get-tuple-element.2), channel_id=1, source_target_pairs={{8,0},{16,8},{24,16},{32,24},{40,32},{48,40},{56,48},{64,56},{72,6... | collective-permute-start | bytes 294920 | tf_op jit(solution)/shard_map/ppermute | solution.py:28
  315.2 10.9 %collective-permute-start.24 = (bf16[1,256,768]{2,1,0:T(8,128)(2,1)S(1)}, bf16[1,256,768]{2,1,0:T(8,128)(2,1)S(1)}, u32[]{:S(2)}, u32[]{:S(2)}) collective-permute-start(bf16[1,256,768]{2,1,0:T(8,128)(2,1)S(1)} %fusion.24), channel_id=1, source_target_pairs={{1,0},{2,1},{3,2},{4,3},{5,4},{6,5},{7,6},{0,7},{9,8},{10,9},{11,1... | collective-permute-start | bytes 1179656 | tf_op jit(solution)/shard_map/ppermute | solution.py:42
